TPU v7x, 512 devices: a whole 4x8x8 slice. The times are simulated.
512 devices in a mesh: win: 8 (over y), lon: 32 (over x, z_lo, core), lat: 2 (over z_hi).
Axes of the slice: x: 4, y: 8, z: 8 (z_hi: 2, z_lo: 4; z = z_hi * 4 + z_lo), core: 2. Of those that a mesh axis runs over, the one named last changes fastest.
Arguments:
- dual_state: float32 [8, 16, 2, 16384], P('win', None, 'lat', 'lon'), may hold values from -6 to 6
- dual_obs: float32 [8, 16, 2, 16384], P('win', None, 'lat', 'lon'), may hold values from -6 to 6
- increment: float32 [8, 16, 2, 16384], P('win', None, 'lat', 'lon'), may hold values from -6 to 6
- resid_dual: float32 [8, 16, 2, 16384], P('win', None, 'lat', 'lon'), may hold values from -6 to 6
- resid_obs: float32 [8, 16, 2, 16384], P('win', None, 'lat', 'lon'), may hold values from -6 to 6
- resid_incr: float32 [8, 16, 2, 16384], P('win', None, 'lat', 'lon'), may hold values from -6 to 6
- search_dual: float32 [8, 16, 2, 16384], P('win', None, 'lat', 'lon'), may hold values from -6 to 6
- search_obs: float32 [8, 16, 2, 16384], P('win', None, 'lat', 'lon'), may hold values from -6 to 6
- search_incr: float32 [8, 16, 2, 16384], P('win', None, 'lat', 'lon'), may hold values from -6 to 6
- ensemble: bfloat16 [8, 64, 16, 2, 16384], P('win', None, None, 'lat', 'lon'), may hold values from -12 to 12
- tangent_coefs: float32 [8, 5, 16, 2, 16384], P('win', None, None, 'lat', 'lon'), may hold values from -0.25 to 0.25
- obs_weight: float32 [8, 16, 2, 16384], P('win', None, 'lat', 'lon'), may hold values from 0.25 to 2
- obs_var: float32 [8, 16, 2, 16384], P('win', None, 'lat', 'lon'), may hold values from 0.5 to 2
- loc_cols: int32 [32, 5], P('lon'), may hold values from 0 to 31, as said below
- loc_vals: bfloat16 [32, 5, 512, 512], P('lon'), may hold values from -0.125 to 0.125
Outputs:
- next_dual: float32 [8, 16, 2, 16384], P('win', None, 'lat', 'lon')
- next_obs: float32 [8, 16, 2, 16384], P('win', None, 'lat', 'lon')
- next_incr: float32 [8, 16, 2, 16384], P('win', None, 'lat', 'lon')
- next_res_dual: float32 [8, 16, 2, 16384], P('win', None, 'lat', 'lon')
- next_res_obs: float32 [8, 16, 2, 16384], P('win', None, 'lat', 'lon')
- next_res_incr: float32 [8, 16, 2, 16384], P('win', None, 'lat', 'lon')
Inputs may be any that keep to these rules, and one draw needn't show every extreme that they name: `loc_cols`: row block i names 5 distinct column blocks, block i itself among them, each within 3 blocks of i around the longitude loop.
All inputs are finite; a program needn't handle non-finite values.
Results may differ from a plain program's by a relative error of at most 0.0017.
Values may be sent and summed in bfloat16 or wider, within the bound.
No kernel may reach another device: no remote copies, remote signals or barrier semaphores. Data moves between devices by JAX's collectives and lax.ppermute only.
A program may use at most 64 MiB of HBM per device.

v0:
```python
import jax
import jax.numpy as jnp
from jax import lax
from jax.sharding import PartitionSpec as P

REACH = 3


def from_offset(value, axis, distance):
    count = lax.axis_size(axis)
    return lax.ppermute(value, axis, [((i + distance) % count, i) for i in range(count)])


def shifted(value, axis, steps):
    count = lax.axis_size(axis)
    leading, last = (max(0, -steps), min(count, count - steps))
    return lax.ppermute(value, axis, [(source, source + steps) for source in range(leading, last)])


def lon_extended(packed, width):
    left = from_offset(packed[..., -width:], "lon", -1)
    right = from_offset(packed[..., :width], "lon", 1)
    return jnp.concatenate([left, packed, right], axis=-1)


def lat_partner(value):
    return lax.ppermute(value, "lat", [(0, 1), (1, 0)])


def forward_pair(f_a, f_b, c_a, cn_a):
    return (
        (0.5 + c_a[0, :, 1:-1]) * f_a[:, 1:-1]
        + c_a[1, :, 1:-1] * f_a[:, 2:]
        + c_a[2, :, 1:-1] * f_a[:, :-2]
        + cn_a[:, 1:-1] * f_b[:, 1:-1]
    )


def adjoint_pair(f_a, f_b, c_a, ca_a):
    return (
        (0.5 + c_a[0, :, 1:-1]) * f_a[:, 1:-1]
        + (c_a[1] * f_a)[:, :-2]
        + (c_a[2] * f_a)[:, 2:]
        + ca_a[:, 1:-1] * f_b[:, 1:-1]
    )


def propagate_both(own, other, first_row):
    u_a, w_a, c_a = (own[0], own[1], own[2:])
    u_b, w_b, c_b = (other[0], other[1], other[2:])
    cn_a = jnp.where(first_row, c_a[3], c_a[4])
    cn_b = jnp.where(first_row, c_b[4], c_b[3])
    ca_a = jnp.where(first_row, c_b[4], c_b[3])
    ca_b = jnp.where(first_row, c_a[3], c_a[4])
    s_a = forward_pair(u_a, u_b, c_a, cn_a)
    s_b = forward_pair(u_b, u_a, c_b, cn_b)
    moved = forward_pair(s_a, s_b, c_a[:, :, 1:-1], cn_a[:, 1:-1])
    t_a = adjoint_pair(w_a, w_b, c_a, ca_a)
    t_b = adjoint_pair(w_b, w_a, c_b, ca_b)
    backed = adjoint_pair(t_a, t_b, c_a[:, :, 1:-1], ca_a[:, 1:-1])
    return (moved, backed)


def localize(members, search, loc_cols, loc_vals):
    count_members = members.shape[0]
    block = members.shape[-1]
    products = (members.astype(jnp.float32) * search[None]).astype(jnp.bfloat16)
    flat = products.reshape(-1, block)
    bands = lax.axis_size("lon")
    here = lax.axis_index("lon")
    columns = loc_cols[0]
    tiles = loc_vals[0]
    offsets = [0]
    for distance in range(1, REACH + 1):
        offsets += [distance, -distance]
    sources = {0: flat}
    for offset in offsets[1:]:
        sources[offset] = from_offset(flat, "lon", offset)

    def weight_for(offset):
        target = (here + offset + bands) % bands
        match = columns == target
        picked = tiles[jnp.argmax(match)]
        return jnp.where(jnp.any(match), picked, jnp.zeros_like(picked))

    total = jnp.dot(flat, weight_for(0), preferred_element_type=jnp.float32)
    for offset in offsets[1:]:
        total = total + jnp.dot(
            sources[offset], weight_for(offset), preferred_element_type=jnp.float32
        )
    spread = total.reshape(products.shape)
    return jnp.sum(members.astype(jnp.float32) * spread, axis=0) / (count_members - 1)


def local(
    dual_state,
    dual_obs,
    increment,
    resid_dual,
    resid_obs,
    resid_incr,
    search_dual,
    search_obs,
    search_incr,
    ensemble,
    tangent_coefs,
    obs_weight,
    obs_var,
    loc_cols,
    loc_vals,
):
    resid_local = (
        jnp.sum(resid_dual * resid_dual)
        + jnp.sum(resid_obs * resid_obs)
        + jnp.sum(resid_incr * resid_incr)
    )
    search_local = (
        jnp.sum(search_dual * search_dual)
        + jnp.sum(search_obs * search_obs)
        + jnp.sum(search_incr * search_incr)
    )
    wide = jnp.broadcast_to(jnp.stack([resid_local, search_local])[:, None], (2, 8192))
    sums = lax.psum(wide, ("win", "lon", "lat"))[:, 0]
    alpha = sums[0] / (sums[1] + 1e-06)
    packed = jnp.concatenate(
        [search_incr[0, :, 0][None], search_dual[0, :, 0][None], tangent_coefs[0, :, :, 0]], axis=0
    )
    own = lon_extended(packed, 2)
    other = lat_partner(own)
    first_row = lax.axis_index("lat") == 0
    moved, backed = propagate_both(own, other, first_row)
    earlier = shifted(moved, "win", 1)[None, :, None]
    following = shifted(backed, "win", -1)[None, :, None]
    covar = localize(ensemble[0, :, :, 0], search_dual[0, :, 0], loc_cols, loc_vals)[None, :, None]
    image_dual = covar + search_incr - earlier
    image_obs = obs_var * search_obs + obs_weight * search_incr
    image_incr = search_dual - following + obs_weight * search_obs
    return (
        dual_state + alpha * search_dual,
        dual_obs + alpha * search_obs,
        increment + alpha * search_incr,
        resid_dual - alpha * image_dual,
        resid_obs - alpha * image_obs,
        resid_incr - alpha * image_incr,
    )


def solution(mesh):
    field = P("win", None, "lat", "lon")
    stacked = P("win", None, None, "lat", "lon")
    placed = (
        field,
        field,
        field,
        field,
        field,
        field,
        field,
        field,
        field,
        stacked,
        stacked,
        field,
        field,
        P("lon", None),
        P("lon", None, None, None),
    )
    return jax.shard_map(local, mesh=mesh, in_specs=placed, out_specs=(field,) * 6, check_vma=False)
```

profile of v0, /device:TPU:8, one launch (start us, length us, event | category | flops | bytes accessed | tf_op | source)
XLA Modules:
  0.0 461.0 jit_solution(7638493862482164467)
XLA Ops:
  7.2 1.5 multiply_reduce_fusion.3
  8.7 1.4 multiply_reduce_fusion
  10.2 1.4 multiply_reduce_fusion.4
  13.6 1.5 multiply_reduce_fusion.1
  17.0 0.7 broadcast_in_dim.6
  17.8 1.4 bitcast_reduce_fusion.3
  19.2 1.3 bitcast_reduce_fusion.4
  20.5 1.3 bitcast_reduce_fusion.5
  21.9 1.3 bitcast_reduce_fusion.1
  23.2 1.3 bitcast_reduce_fusion.2
  24.5 1.3 bitcast_reduce_fusion.6
  25.8 1.4 bitcast_reduce_fusion
  27.2 0.8 fusion.90
  28.0 1.5 compare_reduce_fusion
  38.1 0.9 copy.88
  39.1 0.8 copy.89
  44.2 237.0 %all-reduce.2.cloned.1.call-done = f32[2,8192]{1,0:T(2,128)} async-done(((f32[2,8192]{1,0:T(2,128)}), f32[2,8192]{1,0:T(2,128)}) %all-reduce.2.cloned.1.call-update) | async-done | bytes 65552 | tf_op jit(solution)/shard_map/psum | solution.py:123
  281.2 1.3 fusion.91
  283.8 0.8 copy_bitcast_fusion.4
  284.8 2.5 collective-permute-start.2
  287.3 2.2 collective-permute-start.1
  289.5 7.2 %collective-permute-start = (bf16[1024,512]{1,0:T(8,128)(2,1)S(1)}, bf16[1024,512]{1,0:T(8,128)(2,1)S(1)}, u32[]{:S(2)}, u32[]{:S(2)}) collective-permute-start(bf16[1024,512]{1,0:T(8,128)(2,1)S(1)} %fusion), channel_id=1, source_target_pairs={{2,0},{4,2},{6,4},{8,6},{10,8},{12,10},{14,12},{16,14},{18,16},{20... | collective-permute-start | bytes 3145736 | tf_op jit(solution)/shard_map/ppermute | solution.py:11
  297.1 1.9 collective-permute-start.6
  299.0 7.5 %collective-permute-start.7 = (f32[7,16,2]{2,1,0:T(8,128)S(1)}, f32[7,16,2]{2,1,0:T(8,128)S(1)}, u32[]{:S(2)}, u32[]{:S(2)}) collective-permute-start(f32[7,16,2]{2,1,0:T(8,128)S(1)} %get-tuple-element.51), channel_id=1, source_target_pairs={{2,0},{4,2},{6,4},{8,6},{10,8},{12,10},{14,12},{16,14},{18,16},{20... | collective-permute-start | bytes 2696 | tf_op jit(solution)/shard_map/ppermute | solution.py:11
  306.6 1.4 fusion.17
  308.0 0.6 copy.38
  308.6 25.5 %collective-permute-done.6 = f32[7,16,2]{2,1,0:T(8,128)S(1)} collective-permute-done((f32[7,16,2]{2,1,0:T(8,128)S(1)}, f32[7,16,2]{2,1,0:T(8,128)S(1)}, u32[]{:S(2)}, u32[]{:S(2)}) %collective-permute-start.6) | collective-permute-done | bytes 928 | tf_op jit(solution)/shard_map/ppermute | solution.py:11
  334.1 2.8 collective-permute-start.4
  337.1 7.8 %collective-permute-start.8 = (f32[7,16,516]{2,1,0:T(8,128)S(1)}, f32[7,16,516]{2,1,0:T(8,128)S(1)}, u32[]{:S(2)}, u32[]{:S(2)}) collective-permute-start(f32[7,16,516]{2,1,0:T(8,128)S(1)} %pad_maximum_fusion), channel_id=1, source_target_pairs={{0,1},{1,0},{2,3},{3,2},{4,5},{5,4},{6,7},{7,6},{8,9},{9,8},{10,11... | collective-permute-start | bytes 693512 | tf_op jit(solution)/shard_map/ppermute | solution.py:27
  345.3 32.2 %collective-permute-done.8 = f32[7,16,516]{2,1,0:T(8,128)S(1)} collective-permute-done((f32[7,16,516]{2,1,0:T(8,128)S(1)}, f32[7,16,516]{2,1,0:T(8,128)S(1)}, u32[]{:S(2)}, u32[]{:S(2)}) %collective-permute-start.8) | collective-permute-done | bytes 231200 | tf_op jit(solution)/shard_map/ppermute | solution.py:27
  378.3 1.9 collective-permute-start.10
  380.4 3.7 collective-permute-done.10
  384.1 1.9 collective-permute-start.3
  386.1 0.7 multiply_subtract_fusion
  386.8 1.9 collective-permute-start.5
  388.7 1.4 fusion.11
  390.1 2.2 collective-permute-start.9
  392.3 1.3 fusion.13
  393.6 1.4 fusion.15
  395.0 1.3 fusion.7
  396.4 19.6 %collective-permute-done.3 = bf16[1024,512]{1,0:T(8,128)(2,1)S(1)} collective-permute-done((bf16[1024,512]{1,0:T(8,128)(2,1)S(1)}, bf16[1024,512]{1,0:T(8,128)(2,1)S(1)}, u32[]{:S(2)}, u32[]{:S(2)}) %collective-permute-start.3) | collective-permute-done | bytes 1048608 | tf_op jit(solution)/shard_map/ppermute | solution.py:11
  416.0 1.4 fusion.9
  417.4 31.6 %collective-permute-done.5 = bf16[1024,512]{1,0:T(8,128)(2,1)S(1)} collective-permute-done((bf16[1024,512]{1,0:T(8,128)(2,1)S(1)}, bf16[1024,512]{1,0:T(8,128)(2,1)S(1)}, u32[]{:S(2)}, u32[]{:S(2)}) %collective-permute-start.5) | collective-permute-done | bytes 1048608 | tf_op jit(solution)/shard_map/ppermute | solution.py:11
  449.0 1.6 add_add_fusion
  451.5 0.6 copy.39
  452.2 0.6 copy.40
  452.8 0.6 copy.41
  453.5 0.6 copy.42
  (52 shorter events, 3.0 us)
Async XLA Ops:
  7.2 277.4 %copy-start = (bf16[1,64,16,1,512]{4,2,3,1,0:T(8,128)(2,1)S(1)}, bf16[1,64,16,1,512]{4,2,3,1,0:T(8,128)(2,1)}, u32[]{:S(2)}) copy-start(bf16[1,64,16,1,512]{4,2,3,1,0:T(8,128)(2,1)} %param.24) | copy-start | bytes 3145732
  7.2 274.0 %all-reduce.2.cloned.1.call-start = ((), (), s32[]{:S(2)}) async-start(), calls=%async_computation | async-start | bytes 131072 | tf_op jit(solution)/shard_map/psum | solution.py:123
  284.6 22.0 %copy-start.1 = (bf16[1,5,512,512]{3,2,1,0:T(8,128)(2,1)S(1)}, bf16[1,5,512,512]{3,2,1,0:T(8,128)(2,1)}, u32[]{:S(2)}) copy-start(bf16[1,5,512,512]{3,2,1,0:T(8,128)(2,1)} %param.29) | copy-start | bytes 7864324
  284.8 102.0 %collective-permute-start.2 = (bf16[1024,512]{1,0:T(8,128)(2,1)S(1)}, bf16[1024,512]{1,0:T(8,128)(2,1)S(1)}, u32[]{:S(2)}, u32[]{:S(2)}) collective-permute-start(bf16[1024,512]{1,0:T(8,128)(2,1)S(1)} %fusion), channel_id=1, source_target_pairs={{4,0},{6,2},{8,4},{10,6},{12,8},{14,10},{16,12},{18,14},{20,16},{2... | collective-permute-start | bytes 3145736 | tf_op jit(solution)/shard_map/ppermute | solution.py:11
  287.3 102.8 %collective-permute-start.1 = (bf16[1024,512]{1,0:T(8,128)(2,1)S(1)}, bf16[1024,512]{1,0:T(8,128)(2,1)S(1)}, u32[]{:S(2)}, u32[]{:S(2)}) collective-permute-start(bf16[1024,512]{1,0:T(8,128)(2,1)S(1)} %fusion), channel_id=1, source_target_pairs={{62,0},{0,2},{2,4},{4,6},{6,8},{8,10},{10,12},{12,14},{14,16},{16,... | collective-permute-start | bytes 3145736 | tf_op jit(solution)/shard_map/ppermute | solution.py:11
  289.5 104.1 %collective-permute-start = (bf16[1024,512]{1,0:T(8,128)(2,1)S(1)}, bf16[1024,512]{1,0:T(8,128)(2,1)S(1)}, u32[]{:S(2)}, u32[]{:S(2)}) collective-permute-start(bf16[1024,512]{1,0:T(8,128)(2,1)S(1)} %fusion), channel_id=1, source_target_pairs={{2,0},{4,2},{6,4},{8,6},{10,8},{12,10},{14,12},{16,14},{18,16},{20... | collective-permute-start | bytes 3145736 | tf_op jit(solution)/shard_map/ppermute | solution.py:11
  297.1 37.0 %collective-permute-start.6 = (f32[7,16,2]{2,1,0:T(8,128)S(1)}, f32[7,16,2]{2,1,0:T(8,128)S(1)}, u32[]{:S(2)}, u32[]{:S(2)}) collective-permute-start(f32[7,16,2]{2,1,0:T(8,128)S(1)} %get-tuple-element.50), channel_id=1, source_target_pairs={{62,0},{0,2},{2,4},{4,6},{6,8},{8,10},{10,12},{12,14},{14,16},{16,... | collective-permute-start | bytes 2696 | tf_op jit(solution)/shard_map/ppermute | solution.py:11
  299.0 37.9 %collective-permute-start.7 = (f32[7,16,2]{2,1,0:T(8,128)S(1)}, f32[7,16,2]{2,1,0:T(8,128)S(1)}, u32[]{:S(2)}, u32[]{:S(2)}) collective-permute-start(f32[7,16,2]{2,1,0:T(8,128)S(1)} %get-tuple-element.51), channel_id=1, source_target_pairs={{2,0},{4,2},{6,4},{8,6},{10,8},{12,10},{14,12},{16,14},{18,16},{20... | collective-permute-start | bytes 2696 | tf_op jit(solution)/shard_map/ppermute | solution.py:11
  334.1 60.9 %collective-permute-start.4 = (bf16[1024,512]{1,0:T(8,128)(2,1)S(1)}, bf16[1024,512]{1,0:T(8,128)(2,1)S(1)}, u32[]{:S(2)}, u32[]{:S(2)}) collective-permute-start(bf16[1024,512]{1,0:T(8,128)(2,1)S(1)} %fusion), channel_id=1, source_target_pairs={{6,0},{8,2},{10,4},{12,6},{14,8},{16,10},{18,12},{20,14},{22,16},{... | collective-permute-start | bytes 3145736 | tf_op jit(solution)/shard_map/ppermute | solution.py:11
  337.1 48.9 %copy-start.3 = (f32[1,16,1,512]{3,2,1,0:T(1,128)S(1)}, f32[1,16,1,512]{3,2,1,0:T(1,128)}, u32[]{:S(2)}) copy-start(f32[1,16,1,512]{3,2,1,0:T(1,128)} %param.21) | copy-start | bytes 98308
  337.1 48.9 %copy-start.4 = (f32[1,16,1,512]{3,2,1,0:T(1,128)S(1)}, f32[1,16,1,512]{3,2,1,0:T(1,128)}, u32[]{:S(2)}) copy-start(f32[1,16,1,512]{3,2,1,0:T(1,128)} %param.22) | copy-start | bytes 98308
  337.1 48.9 %copy-start.7 = (f32[1,16,1,512]{3,2,1,0:T(1,128)S(1)}, f32[1,16,1,512]{3,2,1,0:T(1,128)}, u32[]{:S(2)}) copy-start(f32[1,16,1,512]{3,2,1,0:T(1,128)} %param.26) | copy-start | bytes 98308
  337.1 48.9 %copy-start.8 = (f32[1,16,1,512]{3,2,1,0:T(1,128)S(1)}, f32[1,16,1,512]{3,2,1,0:T(1,128)}, u32[]{:S(2)}) copy-start(f32[1,16,1,512]{3,2,1,0:T(1,128)} %param.20) | copy-start | bytes 98308
  337.1 40.3 %collective-permute-start.8 = (f32[7,16,516]{2,1,0:T(8,128)S(1)}, f32[7,16,516]{2,1,0:T(8,128)S(1)}, u32[]{:S(2)}, u32[]{:S(2)}) collective-permute-start(f32[7,16,516]{2,1,0:T(8,128)S(1)} %pad_maximum_fusion), channel_id=1, source_target_pairs={{0,1},{1,0},{2,3},{3,2},{4,5},{5,4},{6,7},{7,6},{8,9},{9,8},{10,11... | collective-permute-start | bytes 693512 | tf_op jit(solution)/shard_map/ppermute | solution.py:27
  378.3 5.8 %collective-permute-start.10 = (f32[16,512]{1,0:T(8,128)S(1)}, f32[16,512]{1,0:T(8,128)S(1)}, u32[]{:S(2)}, u32[]{:S(2)}) collective-permute-start(f32[16,512]{1,0:T(8,128)S(1)} %fusion.59), channel_id=1, source_target_pairs={{64,0},{128,64},{192,128},{256,192},{320,256},{384,320},{448,384},... | collective-permute-start | bytes 98312 | tf_op jit(solution)/shard_map/ppermute | solution.py:17
  384.1 31.9 %collective-permute-start.3 = (bf16[1024,512]{1,0:T(8,128)(2,1)S(1)}, bf16[1024,512]{1,0:T(8,128)(2,1)S(1)}, u32[]{:S(2)}, u32[]{:S(2)}) collective-permute-start(bf16[1024,512]{1,0:T(8,128)(2,1)S(1)} %fusion), channel_id=1, source_target_pairs={{60,0},{62,2},{0,4},{2,6},{4,8},{6,10},{8,12},{10,14},{12,16},{14,... | collective-permute-start | bytes 3145736 | tf_op jit(solution)/shard_map/ppermute | solution.py:11
  386.8 62.2 %collective-permute-start.5 = (bf16[1024,512]{1,0:T(8,128)(2,1)S(1)}, bf16[1024,512]{1,0:T(8,128)(2,1)S(1)}, u32[]{:S(2)}, u32[]{:S(2)}) collective-permute-start(bf16[1024,512]{1,0:T(8,128)(2,1)S(1)} %fusion), channel_id=1, source_target_pairs={{58,0},{60,2},{62,4},{0,6},{2,8},{4,10},{6,12},{8,14},{10,16},{12,... | collective-permute-start | bytes 3145736 | tf_op jit(solution)/shard_map/ppermute | solution.py:11
  390.1 61.0 %collective-permute-start.9 = (f32[16,512]{1,0:T(8,128)S(1)}, f32[16,512]{1,0:T(8,128)S(1)}, u32[]{:S(2)}, u32[]{:S(2)}) collective-permute-start(f32[16,512]{1,0:T(8,128)S(1)} %fusion.66), channel_id=1, source_target_pairs={{0,64},{64,128},{128,192},{192,256},{256,320},{320,384},{384,448},... | collective-permute-start | bytes 98312 | tf_op jit(solution)/shard_map/ppermute | solution.py:17
  450.6 0.8 copy-start.2
  450.7 0.8 copy-start.5
  450.7 0.8 copy-start.6
  450.7 0.8 copy-start.9
  450.7 0.8 copy-start.10
  450.7 0.8 copy-start.11
Sparse Core Ops, SparseCore 0:
  17.9 263.2 all-reduce.1
where the time goes:
time: 462 us; the launch traced here: 461 us
  waiting for transfers between devices  350 us (76%)
  starting transfers between devices  40 us (9%)
  between operations  32.7 us (7%)
  other arithmetic  20 us (4%)
  matrix products  9.73 us (2%)
  local copies, waits for them, and re-layouts  8.71 us (2%)
    psum x1, waiting for transfers between devices, local(): sums = lax.psum(wide, ('win', 'lon', 'lat'))[:, 0]  237 us
    ppermute x8, waiting for transfers between devices, from_offset(): lax.ppermute(value, axis, [((i + distance) % count, i) for i in range(cou...  76.8 us
    ppermute x1, waiting for transfers between devices, lat_partner(): return lax.ppermute(value, 'lat', [(0, 1), (1, 0)])  32.2 us
    ppermute x8, starting transfers between devices, from_offset(): lax.ppermute(value, axis, [((i + distance) % count, i) for i in range(cou...  28 us
    another operation x7, other arithmetic, weight_for(): picked = tiles[jnp.argmax(match)]  9.35 us
  transfers between devices with their start and end apart: 12, of which 6 were waited for; matrix products, arithmetic and copies ran while one was open for 6% of the time, Pallas kernels for 0%

commit v1 on v0

--- a/solution.py
+++ b/solution.py
@@ -120,7 +120,7 @@
         + jnp.sum(search_incr * search_incr)
     )
     wide = jnp.broadcast_to(jnp.stack([resid_local, search_local])[:, None], (2, 8192))
-    sums = lax.psum(wide, ("win", "lon", "lat"))[:, 0]
+    sums = jnp.sum(lax.all_gather(wide, ("win", "lon", "lat")), axis=0)[:, 0]
     alpha = sums[0] / (sums[1] + 1e-06)
     packed = jnp.concatenate(
         [search_incr[0, :, 0][None], search_dual[0, :, 0][None], tangent_coefs[0, :, :, 0]], axis=0

time: 462 us -> 290 us (0.63)
  the two profiles are of different devices: /device:TPU:8 before, /device:TPU:24 now
where the time goes in v1:
time: 290 us; the launch traced here: 289 us
  blocking collectives  105 us (36%)
  waiting for transfers between devices  87.3 us (30%)
  starting transfers between devices  37.7 us (13%)
  other arithmetic  19.9 us (7%)
  between operations  19.9 us (7%)
  matrix products  14.7 us (5%)
  local copies, waits for them, and re-layouts  5.1 us (2%)
    unnamed x1, blocking collectives  105 us
    ppermute x8, waiting for transfers between devices, from_offset(): lax.ppermute(value, axis, [((i + distance) % count, i) for i in range(cou...  51.2 us
    ppermute x1, waiting for transfers between devices, lat_partner(): return lax.ppermute(value, 'lat', [(0, 1), (1, 0)])  31.3 us
    ppermute x8, starting transfers between devices, from_offset(): lax.ppermute(value, axis, [((i + distance) % count, i) for i in range(cou...  26.9 us
    dot_general x6, matrix products, localize(): jnp.dot(sources[offset], weight_for(offset), preferred_element_type=jnp.f...  12 us
  transfers between devices with their start and end apart: 11, of which 5 were waited for; matrix products, arithmetic and copies ran while one was open for 9% of the time, Pallas kernels for 0%

profile of v1, /device:TPU:24, one launch (start us, length us, event | category | flops | bytes accessed | tf_op | source)
XLA Modules:
  0.0 289.1 jit_solution(6220484373274836380)
XLA Ops:
  0.7 1.5 multiply_reduce_fusion.3
  2.2 1.4 multiply_reduce_fusion
  3.6 1.4 multiply_reduce_fusion.4
  7.0 1.5 multiply_reduce_fusion.1
  10.6 104.6 %all-reduce = f32[1024]{0:T(1024)S(1)} all-reduce(f32[1024]{0:T(1024)S(1)} %maximum_dynamic-update-slice_fusion), channel_id=3, replica_groups=mesh['win'=8,'lon'=32,'lat'=2] {'win','lon','lat'}, use_global_device_ids=true, to_apply=%add | all-reduce | flops 1024 | bytes 8192
  115.9 0.5 fusion.91
  117.7 0.8 copy_bitcast_fusion.4
  118.5 2.4 fusion
  120.9 1.9 collective-permute-start.2
  122.8 1.9 collective-permute-start.1
  124.7 7.6 %collective-permute-start = (bf16[1024,512]{1,0:T(8,128)(2,1)}, bf16[1024,512]{1,0:T(8,128)(2,1)}, u32[]{:S(2)}, u32[]{:S(2)}) collective-permute-start(bf16[1024,512]{1,0:T(8,128)(2,1)} %fusion), channel_id=1, source_target_pairs={{2,0},{4,2},{6,4},{8,6},{10,8},{12,10},{14,12},{16,14},{18,16},{20... | collective-permute-start | bytes 3145736 | tf_op jit(solution)/shard_map/ppermute | solution.py:11
  132.4 0.7 pad_maximum_fusion.3
  133.1 1.9 collective-permute-start.6
  135.0 7.6 %collective-permute-start.7 = (f32[7,16,2]{2,1,0:T(8,128)}, f32[7,16,2]{2,1,0:T(8,128)}, u32[]{:S(2)}, u32[]{:S(2)}) collective-permute-start(f32[7,16,2]{2,1,0:T(8,128)} %get-tuple-element.63), channel_id=1, source_target_pairs={{2,0},{4,2},{6,4},{8,6},{10,8},{12,10},{14,12},{16,14},{18,16},{20... | collective-permute-start | bytes 2696 | tf_op jit(solution)/shard_map/ppermute | solution.py:11
  142.6 0.7 bitcast_reduce_fusion.3
  144.7 0.7 bitcast_reduce_fusion.4
  146.5 0.7 bitcast_reduce_fusion.5
  148.5 0.7 bitcast_reduce_fusion.6
  150.4 1.2 fusion.1
  151.7 0.7 bitcast_reduce_fusion.1
  152.3 0.7 bitcast_reduce_fusion.2
  153.0 0.8 compare_reduce_fusion
  153.8 0.7 bitcast_reduce_fusion
  155.8 2.7 fusion.17
  161.9 0.6 copy.83
  166.3 4.1 %collective-permute-done.6 = f32[7,16,2]{2,1,0:T(8,128)} collective-permute-done((f32[7,16,2]{2,1,0:T(8,128)}, f32[7,16,2]{2,1,0:T(8,128)}, u32[]{:S(2)}, u32[]{:S(2)}) %collective-permute-start.6) | collective-permute-done | bytes 928 | tf_op jit(solution)/shard_map/ppermute | solution.py:11
  170.5 2.2 collective-permute-start.4
  172.7 1.0 pad_maximum_fusion
  173.8 5.6 %collective-permute-start.8 = (f32[7,16,516]{2,1,0:T(8,128)S(1)}, f32[7,16,516]{2,1,0:T(8,128)S(1)}, u32[]{:S(2)}, u32[]{:S(2)}) collective-permute-start(f32[7,16,516]{2,1,0:T(8,128)S(1)} %pad_maximum_fusion), channel_id=1, source_target_pairs={{0,1},{1,0},{2,3},{3,2},{4,5},{5,4},{6,7},{7,6},{8,9},{9,8},{10,11... | collective-permute-start | bytes 693512 | tf_op jit(solution)/shard_map/ppermute | solution.py:27
  179.7 31.3 %collective-permute-done.8 = f32[7,16,516]{2,1,0:T(8,128)S(1)} collective-permute-done((f32[7,16,516]{2,1,0:T(8,128)S(1)}, f32[7,16,516]{2,1,0:T(8,128)S(1)}, u32[]{:S(2)}, u32[]{:S(2)}) %collective-permute-start.8) | collective-permute-done | bytes 231200 | tf_op jit(solution)/shard_map/ppermute | solution.py:27
  211.8 2.0 collective-permute-start.10
  214.0 4.8 %collective-permute-done.10 = f32[16,512]{1,0:T(8,128)S(1)} collective-permute-done((f32[16,512]{1,0:T(8,128)S(1)}, f32[16,512]{1,0:T(8,128)S(1)}, u32[]{:S(2)}, u32[]{:S(2)}) %collective-permute-start.10) | collective-permute-done | bytes 32800 | tf_op jit(solution)/shard_map/ppermute | solution.py:17
  218.8 1.9 collective-permute-start.3
  220.8 0.7 multiply_subtract_fusion
  221.5 1.9 collective-permute-start.5
  223.4 2.6 fusion.11
  226.0 3.2 %collective-permute-start.9 = (f32[16,512]{1,0:T(8,128)S(1)}, f32[16,512]{1,0:T(8,128)S(1)}, u32[]{:S(2)}, u32[]{:S(2)}) collective-permute-start(f32[16,512]{1,0:T(8,128)S(1)} %fusion.66), channel_id=1, source_target_pairs={{0,64},{64,128},{128,192},{192,256},{256,320},{320,384},{384,448},... | collective-permute-start | bytes 98312 | tf_op jit(solution)/shard_map/ppermute | solution.py:17
  229.2 2.6 fusion.13
  231.8 2.5 fusion.15
  234.3 1.4 fusion.7
  235.7 15.2 %collective-permute-done.3 = bf16[1024,512]{1,0:T(8,128)(2,1)S(1)} collective-permute-done((bf16[1024,512]{1,0:T(8,128)(2,1)}, bf16[1024,512]{1,0:T(8,128)(2,1)S(1)}, u32[]{:S(2)}, u32[]{:S(2)}) %collective-permute-start.3) | collective-permute-done | bytes 1048608 | tf_op jit(solution)/shard_map/ppermute | solution.py:11
  250.9 1.4 fusion.9
  252.2 31.8 %collective-permute-done.5 = bf16[1024,512]{1,0:T(8,128)(2,1)S(1)} collective-permute-done((bf16[1024,512]{1,0:T(8,128)(2,1)}, bf16[1024,512]{1,0:T(8,128)(2,1)S(1)}, u32[]{:S(2)}, u32[]{:S(2)}) %collective-permute-start.5) | collective-permute-done | bytes 1048608 | tf_op jit(solution)/shard_map/ppermute | solution.py:11
  284.0 1.6 add_add_fusion
  286.5 0.6 copy.84
  287.2 0.6 copy.85
  287.8 0.6 copy.86
  288.5 0.6 copy.87
  (57 shorter events, 2.9 us)
Async XLA Ops:
  0.6 131.7 %copy-start.3 = (f32[1,16,1,512]{3,2,1,0:T(1,128)S(1)}, f32[1,16,1,512]{3,2,1,0:T(1,128)}, u32[]{:S(2)}) copy-start(f32[1,16,1,512]{3,2,1,0:T(1,128)} %param.23) | copy-start | bytes 98308
  0.6 149.8 %copy-start = (bf16[1,64,16,1,512]{4,2,3,1,0:T(8,128)(2,1)S(1)}, bf16[1,64,16,1,512]{4,2,3,1,0:T(8,128)(2,1)}, u32[]{:S(2)}) copy-start(bf16[1,64,16,1,512]{4,2,3,1,0:T(8,128)(2,1)} %param.24) | copy-start | bytes 3145732
  0.7 131.7 %copy-start.2 = (f32[1,5,16,1,512]{4,3,2,1,0:T(1,128)S(1)}, f32[1,5,16,1,512]{4,3,2,1,0:T(1,128)}, u32[]{:S(2)}) copy-start(f32[1,5,16,1,512]{4,3,2,1,0:T(1,128)} %param.25) | copy-start | bytes 491524
  0.7 141.9 %copy-start.13 = (s32[1,5]{1,0:T(1,128)S(1)}, s32[1,5]{1,0:T(1,128)}, u32[]{:S(2)}) copy-start(s32[1,5]{1,0:T(1,128)} %param.28) | copy-start | bytes 64
  120.9 100.6 %collective-permute-start.2 = (bf16[1024,512]{1,0:T(8,128)(2,1)}, bf16[1024,512]{1,0:T(8,128)(2,1)}, u32[]{:S(2)}, u32[]{:S(2)}) collective-permute-start(bf16[1024,512]{1,0:T(8,128)(2,1)} %fusion), channel_id=1, source_target_pairs={{4,0},{6,2},{8,4},{10,6},{12,8},{14,10},{16,12},{18,14},{20,16},{2... | collective-permute-start | bytes 3145736 | tf_op jit(solution)/shard_map/ppermute | solution.py:11
  122.8 103.1 %collective-permute-start.1 = (bf16[1024,512]{1,0:T(8,128)(2,1)}, bf16[1024,512]{1,0:T(8,128)(2,1)}, u32[]{:S(2)}, u32[]{:S(2)}) collective-permute-start(bf16[1024,512]{1,0:T(8,128)(2,1)} %fusion), channel_id=1, source_target_pairs={{62,0},{0,2},{2,4},{4,6},{6,8},{8,10},{10,12},{12,14},{14,16},{16,... | collective-permute-start | bytes 3145736 | tf_op jit(solution)/shard_map/ppermute | solution.py:11
  124.7 107.0 %collective-permute-start = (bf16[1024,512]{1,0:T(8,128)(2,1)}, bf16[1024,512]{1,0:T(8,128)(2,1)}, u32[]{:S(2)}, u32[]{:S(2)}) collective-permute-start(bf16[1024,512]{1,0:T(8,128)(2,1)} %fusion), channel_id=1, source_target_pairs={{2,0},{4,2},{6,4},{8,6},{10,8},{12,10},{14,12},{16,14},{18,16},{20... | collective-permute-start | bytes 3145736 | tf_op jit(solution)/shard_map/ppermute | solution.py:11
  133.1 37.4 %collective-permute-start.6 = (f32[7,16,2]{2,1,0:T(8,128)}, f32[7,16,2]{2,1,0:T(8,128)}, u32[]{:S(2)}, u32[]{:S(2)}) collective-permute-start(f32[7,16,2]{2,1,0:T(8,128)} %get-tuple-element.62), channel_id=1, source_target_pairs={{62,0},{0,2},{2,4},{4,6},{6,8},{8,10},{10,12},{12,14},{14,16},{16,... | collective-permute-start | bytes 2696 | tf_op jit(solution)/shard_map/ppermute | solution.py:11
  135.0 37.7 %collective-permute-start.7 = (f32[7,16,2]{2,1,0:T(8,128)}, f32[7,16,2]{2,1,0:T(8,128)}, u32[]{:S(2)}, u32[]{:S(2)}) collective-permute-start(f32[7,16,2]{2,1,0:T(8,128)} %get-tuple-element.63), channel_id=1, source_target_pairs={{2,0},{4,2},{6,4},{8,6},{10,8},{12,10},{14,12},{16,14},{18,16},{20... | collective-permute-start | bytes 2696 | tf_op jit(solution)/shard_map/ppermute | solution.py:11
  170.5 63.8 %collective-permute-start.4 = (bf16[1024,512]{1,0:T(8,128)(2,1)}, bf16[1024,512]{1,0:T(8,128)(2,1)S(1)}, u32[]{:S(2)}, u32[]{:S(2)}) collective-permute-start(bf16[1024,512]{1,0:T(8,128)(2,1)} %fusion), channel_id=1, source_target_pairs={{6,0},{8,2},{10,4},{12,6},{14,8},{16,10},{18,12},{20,14},{22,16},{... | collective-permute-start | bytes 3145736 | tf_op jit(solution)/shard_map/ppermute | solution.py:11
  173.7 47.0 %copy-start.4 = (f32[1,16,1,512]{3,2,1,0:T(1,128)S(1)}, f32[1,16,1,512]{3,2,1,0:T(1,128)}, u32[]{:S(2)}) copy-start(f32[1,16,1,512]{3,2,1,0:T(1,128)} %param.21) | copy-start | bytes 98308
  173.7 47.0 %copy-start.5 = (f32[1,16,1,512]{3,2,1,0:T(1,128)S(1)}, f32[1,16,1,512]{3,2,1,0:T(1,128)}, u32[]{:S(2)}) copy-start(f32[1,16,1,512]{3,2,1,0:T(1,128)} %param.22) | copy-start | bytes 98308
  173.8 47.0 %copy-start.8 = (f32[1,16,1,512]{3,2,1,0:T(1,128)S(1)}, f32[1,16,1,512]{3,2,1,0:T(1,128)}, u32[]{:S(2)}) copy-start(f32[1,16,1,512]{3,2,1,0:T(1,128)} %param.26) | copy-start | bytes 98308
  173.8 47.0 %copy-start.9 = (f32[1,16,1,512]{3,2,1,0:T(1,128)S(1)}, f32[1,16,1,512]{3,2,1,0:T(1,128)}, u32[]{:S(2)}) copy-start(f32[1,16,1,512]{3,2,1,0:T(1,128)} %param.20) | copy-start | bytes 98308
  173.8 49.6 %copy-start.1 = (bf16[1,5,512,512]{3,2,1,0:T(8,128)(2,1)S(1)}, bf16[1,5,512,512]{3,2,1,0:T(8,128)(2,1)}, u32[]{:S(2)}) copy-start(bf16[1,5,512,512]{3,2,1,0:T(8,128)(2,1)} %param.29) | copy-start | bytes 7864324
  173.8 37.1 %collective-permute-start.8 = (f32[7,16,516]{2,1,0:T(8,128)S(1)}, f32[7,16,516]{2,1,0:T(8,128)S(1)}, u32[]{:S(2)}, u32[]{:S(2)}) collective-permute-start(f32[7,16,516]{2,1,0:T(8,128)S(1)} %pad_maximum_fusion), channel_id=1, source_target_pairs={{0,1},{1,0},{2,3},{3,2},{4,5},{5,4},{6,7},{7,6},{8,9},{9,8},{10,11... | collective-permute-start | bytes 693512 | tf_op jit(solution)/shard_map/ppermute | solution.py:27
  211.8 7.0 %collective-permute-start.10 = (f32[16,512]{1,0:T(8,128)S(1)}, f32[16,512]{1,0:T(8,128)S(1)}, u32[]{:S(2)}, u32[]{:S(2)}) collective-permute-start(f32[16,512]{1,0:T(8,128)S(1)} %fusion.59), channel_id=1, source_target_pairs={{64,0},{128,64},{192,128},{256,192},{320,256},{384,320},{448,384},... | collective-permute-start | bytes 98312 | tf_op jit(solution)/shard_map/ppermute | solution.py:17
  218.8 32.1 %collective-permute-start.3 = (bf16[1024,512]{1,0:T(8,128)(2,1)}, bf16[1024,512]{1,0:T(8,128)(2,1)S(1)}, u32[]{:S(2)}, u32[]{:S(2)}) collective-permute-start(bf16[1024,512]{1,0:T(8,128)(2,1)} %fusion), channel_id=1, source_target_pairs={{60,0},{62,2},{0,4},{2,6},{4,8},{6,10},{8,12},{10,14},{12,16},{14,... | collective-permute-start | bytes 3145736 | tf_op jit(solution)/shard_map/ppermute | solution.py:11
  221.5 62.6 %collective-permute-start.5 = (bf16[1024,512]{1,0:T(8,128)(2,1)}, bf16[1024,512]{1,0:T(8,128)(2,1)S(1)}, u32[]{:S(2)}, u32[]{:S(2)}) collective-permute-start(bf16[1024,512]{1,0:T(8,128)(2,1)} %fusion), channel_id=1, source_target_pairs={{58,0},{60,2},{62,4},{0,6},{2,8},{4,10},{6,12},{8,14},{10,16},{12,... | collective-permute-start | bytes 3145736 | tf_op jit(solution)/shard_map/ppermute | solution.py:11
  226.0 60.2 %collective-permute-start.9 = (f32[16,512]{1,0:T(8,128)S(1)}, f32[16,512]{1,0:T(8,128)S(1)}, u32[]{:S(2)}, u32[]{:S(2)}) collective-permute-start(f32[16,512]{1,0:T(8,128)S(1)} %fusion.66), channel_id=1, source_target_pairs={{0,64},{64,128},{128,192},{192,256},{256,320},{320,384},{384,448},... | collective-permute-start | bytes 98312 | tf_op jit(solution)/shard_map/ppermute | solution.py:17
  285.7 0.8 copy-start.6
  285.7 0.8 copy-start.7
  285.7 0.8 copy-start.10
  285.7 0.8 copy-start.11
  285.7 0.8 copy-start.12
